TPU v7x, 256 devices: a whole 4x4x8 slice. The times are simulated.
256 devices in a mesh: cent: 8 (over z), dp: 32 (over x, y, core).
Axes of the slice: x: 4, y: 4, z: 8, core: 2. Of those that a mesh axis runs over, the one named last changes fastest.
Arguments:
- points: bfloat16 [32768, 1024], P('dp'), may hold values from -6 to 6
- cluster_ids: int32 [32768, 1], P('dp'), may hold values from 0 to 63; in each aligned block of 1024 rows (0 to 1023, 1024 to 2047, ...) at most 64 rows name the same one
- centroids: bfloat16 [8192, 1024], P('cent'), may hold values from -6 to 6
- sub_centroids: bfloat16 [64, 1024, 1024], P('dp', 'cent'), may hold values from -6 to 6
Outputs:
- assign: bfloat16 [32768, 8192], P('dp', 'cent')
- sub_assign: bfloat16 [32768, 1024], P('dp', 'cent')
Inputs may be any that keep to these rules, and one draw needn't show every extreme that they name: `cluster_ids`: among the 1024 points of one index of dp, no level-two cluster holds more than 64 points; some cluster holds exactly 64 in some block.
All inputs are finite; a program needn't handle non-finite values.
Results may differ from a plain program's by a relative error of at most 0.001.
Values may be sent and summed in bfloat16 or wider, within the bound.
No kernel may reach another device: no remote copies, remote signals or barrier semaphores. Data moves between devices by JAX's collectives and lax.ppermute only.
A program may use at most 128 MiB of HBM per device.

v0:
```python
import jax
import jax.numpy as jnp
from jax import lax
from jax.sharding import PartitionSpec as P

CAP = 64
ITERS = 3
EPS = 1e-06
TAU = 0.05


def inverse_norm(rows):
    values = rows.astype(jnp.float32)
    return lax.rsqrt(jnp.mean(values * values, axis=-1) + EPS)


def shards(points, cluster_ids, centroids, sub_centroids):
    pts_count = points.shape[0]
    width = points.shape[1]
    dp_count = lax.axis_size("dp")
    cent_count = lax.axis_size("cent")
    group_dev = sub_centroids.shape[0]
    sub_dev = sub_centroids.shape[1]
    clusters = group_dev * dp_count
    total_cent = centroids.shape[0] * cent_count
    total_sub = sub_dev * cent_count
    inv_x = inverse_norm(points)
    inv_c = inverse_norm(centroids)
    inv_u = inverse_norm(sub_centroids)
    scores = jnp.einsum("pd,kd->pk", points, centroids, preferred_element_type=jnp.float32)
    expo = jnp.exp(scores * inv_x[:, None] * inv_c[None, :] * (1.0 / (width * TAU)))
    row_scale = jnp.ones((pts_count,), jnp.float32)
    col_scale = jnp.ones((centroids.shape[0],), jnp.float32)
    row_part = row_scale
    for step in range(ITERS):
        col_part = jnp.dot(row_scale, expo, precision=lax.Precision.HIGHEST)
        col_scale = 1.0 / lax.psum(col_part, "dp")
        row_part = jnp.dot(expo, col_scale, precision=lax.Precision.HIGHEST)
        if step + 1 < ITERS:
            row_scale = 1.0 / lax.psum(row_part, "cent")
    ids = cluster_ids[:, 0]
    labels = lax.broadcasted_iota(jnp.int32, (pts_count, clusters), 1)
    onehot = ids[:, None] == labels
    positions = lax.broadcasted_iota(jnp.int32, (pts_count, pts_count), 0)
    earlier = (positions > positions.T).astype(jnp.bfloat16)
    before = jnp.dot(earlier, onehot.astype(jnp.bfloat16), preferred_element_type=jnp.float32)
    rank = jnp.sum(before * onehot.astype(jnp.float32), axis=1).astype(jnp.int32)
    slot = ids * CAP + rank
    buffer = jnp.zeros((clusters * CAP, width), jnp.bfloat16).at[slot].set(points)
    scale_two = 1.0 / (width * TAU)
    outgoing = buffer.reshape(dp_count, group_dev * CAP, width)
    arrived = lax.all_to_all(outgoing, "dp", split_axis=0, concat_axis=0, tiled=True)
    arrived = arrived.reshape(dp_count, group_dev, CAP, width)
    inv_rows = inverse_norm(arrived)
    dots = jnp.einsum("sgcd,gkd->sgck", arrived, sub_centroids, preferred_element_type=jnp.float32)
    weights = jnp.exp(dots * inv_rows[..., None] * inv_u[None, :, None, :] * scale_two)
    weights = weights.reshape(dp_count, group_dev * CAP, sub_dev)
    returned = lax.all_to_all(weights, "dp", split_axis=0, concat_axis=0, tiled=True)
    slot_weights = returned.reshape(clusters * CAP, sub_dev)
    point_weights = slot_weights[slot]
    denom_part = jnp.sum(point_weights, axis=1)
    row_total = lax.psum(row_part, "cent")
    denominator = lax.psum(denom_part, "cent")
    row_scale = 1.0 / row_total
    assign = (expo * row_scale[:, None] * col_scale[None, :] * total_cent).astype(jnp.bfloat16)
    sub_assign = (total_sub * point_weights / denominator[:, None]).astype(jnp.bfloat16)
    return (assign, sub_assign)


def solution(mesh):
    return jax.shard_map(
        shards,
        mesh=mesh,
        in_specs=(P("dp", None), P("dp", None), P("cent", None), P("dp", "cent", None)),
        out_specs=(P("dp", "cent"), P("dp", "cent")),
        check_vma=False,
    )
```

profile of v0, /device:TPU:0, one launch (start us, length us, event | category | flops | bytes accessed | tf_op | source)
XLA Modules:
  0.0 412.9 jit_solution(17542967821555174308)
XLA Ops:
  0.6 1.4 fusion.11
  2.0 0.7 compare_select_fusion
  2.7 10.8 %scatter_custom_fusion = bf16[4096,1024]{1,0:T(8,128)(2,1)} fusion(s32[1024]{0:T(1024)S(1)} %bitcast.56, bf16[1024,1024]{1,0:T(8,128)(2,1)} %param.4, bf16[]{:T(256)} %constant.6.clone.1), kind=kCustom, calls=%fused_computation.6 | custom fusion | bytes 8389120 | tf_op jit(solution)/shard_map/scatter | solution.py:49
  13.5 0.0 copy-start.1
  13.5 6.1 %all-to-all-start = ((bf16[32,128,1024]{2,1,0:T(8,128)(2,1)}), bf16[32,128,1024]{2,1,0:T(8,128)(2,1)}, u32[]{:S(2)}, u32[]{:S(2)}) async-start(bf16[32,128,1024]{2,1,0:T(8,128)(2,1)} %bitcast.51), calls=%async_computation | async-start | bytes 16777216 | tf_op jit(solution)/shard_map/all_to_all | solution.py:52
  19.6 0.0 copy-start.2
  19.6 2.2 multiply_reduce_fusion.1
  21.8 0.0 copy-done.1
  21.8 0.5 multiply_reduce_fusion.2
  22.3 0.0 copy-done.2
  22.3 2.6 multiply_exponential_fusion
  24.9 0.0 copy-start
  24.9 1.9 copy-done
  26.9 0.0 copy-start.3
  26.9 2.1 fusion.14
  28.9 141.6 %psum.49 = f32[1024]{0:T(1024)S(1)} all-reduce(f32[1024]{0:T(1024)S(1)} %bitcast.55), channel_id=1, replica_groups=mesh['cent'=8,'dp'=32] {'dp'}, use_global_device_ids=true, to_apply=%region_2.0 | all-reduce | flops 1024 | bytes 8192 | tf_op jit(solution)/shard_map/psum | solution.py:37
  170.5 5.8 %fusion.17 = f32[1,1024]{1,0:T(1,128)S(1)} fusion(f32[1024,1024]{1,0:T(8,128)} %copy-done, f32[1024,1]{0,1:T(1,128)S(1)} %bitcast.61), kind=kOutput, calls=%fused_computation.39 | convolution fusion | flops 12582912 | bytes 4202496 | tf_op jit(solution)/shard_map/dot_general | solution.py:38
  176.3 20.0 %psum.50 = f32[1024]{0:T(1024)S(1)} all-reduce(f32[1024]{0:T(1024)S(1)} %bitcast.62), channel_id=1, replica_groups=mesh['cent'=8,'dp'=32] {'cent'}, use_global_device_ids=true, to_apply=%region_3.0 | all-reduce | flops 1024 | bytes 8192 | tf_op jit(solution)/shard_map/psum | solution.py:40
  196.3 0.0 copy-done.3
  196.3 0.2 multiply_reduce_fusion.3
  196.5 0.0 all-to-all-done
  196.5 5.1 %multiply_reduce_fusion = f32[32,128]{1,0:T(8,128)S(1)} fusion(bf16[32,128,1024]{2,1,0:T(8,128)(2,1)} %all-to-all-done), kind=kLoop, calls=%fused_computation.2 | loop fusion | flops 12578816 | bytes 8404992 | tf_op jit(solution)/shard_map/reduce_sum | solution.py:14
  201.6 0.1 rsqrt.34
  201.7 4.8 %fusion.7 = f32[32,2,64,128]{3,2,0,1:T(8,128)S(1)} fusion(bf16[32,2,64,1024]{3,2,1,0:T(8,128)(2,1)} %bitcast.16, f32[2,128]{1,0:T(2,128)S(1)} %add_rsqrt_fusion.3, f32[32,2,64]{2,0,1:T(8,128)S(1)} %copy.7, bf16[2,128,1024]{2,1,0:T(8,128)(2,1)S(1)} %copy-done.3), kind=kOutput, calls=%fused_computation.16 | convolution fusion | flops 1075314688 | bytes 11027456 | tf_op jit(solution)/shard_map/sgcd,gkd->sgck/dot_general | solution.py:55
  206.5 1.5 copy.8
  208.0 5.4 %all-to-all-start.1 = ((f32[32,128,128]{2,1,0:T(8,128)}), f32[32,128,128]{2,1,0:T(8,128)S(1)}, u32[]{:S(2)}, u32[]{:S(2)}) async-start(f32[32,128,128]{2,1,0:T(8,128)} %bitcast.53), calls=%async_computation.1 | async-start | bytes 4194304 | tf_op jit(solution)/shard_map/all_to_all | solution.py:58
  213.4 4.3 %fusion.18 = f32[1,1024]{1,0:T(1,128)S(1)} fusion(f32[1024,1]{0,1:T(1,128)S(1)} %bitcast.59, f32[1024,1024]{1,0:T(8,128)} %copy-done), kind=kOutput, calls=%fused_computation.40 | convolution fusion | flops 12582912 | bytes 4202496 | tf_op jit(solution)/shard_map/dot_general | solution.py:36
  217.6 78.1 %psum.51 = f32[1024]{0:T(1024)S(1)} all-reduce(f32[1024]{0:T(1024)S(1)} %bitcast.63), channel_id=1, replica_groups=mesh['cent'=8,'dp'=32] {'dp'}, use_global_device_ids=true, to_apply=%region_4.0 | all-reduce | flops 1024 | bytes 8192 | tf_op jit(solution)/shard_map/psum | solution.py:37
  295.7 5.8 %fusion.19 = f32[1,1024]{1,0:T(1,128)S(1)} fusion(f32[1024,1024]{1,0:T(8,128)} %copy-done, f32[1024,1]{0,1:T(1,128)S(1)} %bitcast.64), kind=kOutput, calls=%fused_computation.41 | convolution fusion | flops 12582912 | bytes 4202496 | tf_op jit(solution)/shard_map/dot_general | solution.py:38
  301.5 14.2 %psum.52 = f32[1024]{0:T(1024)S(1)} all-reduce(f32[1024]{0:T(1024)S(1)} %bitcast.65), channel_id=1, replica_groups=mesh['cent'=8,'dp'=32] {'cent'}, use_global_device_ids=true, to_apply=%region_5.0 | all-reduce | flops 1024 | bytes 8192 | tf_op jit(solution)/shard_map/psum | solution.py:40
  315.7 4.3 %fusion.20 = f32[1,1024]{1,0:T(1,128)S(1)} fusion(f32[1024,1]{0,1:T(1,128)S(1)} %bitcast.66, f32[1024,1024]{1,0:T(8,128)} %copy-done), kind=kOutput, calls=%fused_computation.42 | convolution fusion | flops 12582912 | bytes 4202496 | tf_op jit(solution)/shard_map/dot_general | solution.py:36
  319.9 62.7 %psum.53 = f32[1024]{0:T(1024)S(1)} all-reduce(f32[1024]{0:T(1024)S(1)} %bitcast.67), channel_id=1, replica_groups=mesh['cent'=8,'dp'=32] {'dp'}, use_global_device_ids=true, to_apply=%region_6.0 | all-reduce | flops 1024 | bytes 8192 | tf_op jit(solution)/shard_map/psum | solution.py:37
  382.6 5.8 %fusion.21 = f32[1,1024]{1,0:T(1,128)S(1)} fusion(f32[1024,1024]{1,0:T(8,128)} %copy-done, f32[1024,1]{0,1:T(1,128)S(1)} %bitcast.54), kind=kOutput, calls=%fused_computation.43 | convolution fusion | flops 12582912 | bytes 4202496 | tf_op jit(solution)/shard_map/dot_general | solution.py:38
  388.4 0.0 all-to-all-done.1
  388.4 2.8 gather_fusion
  391.2 0.2 reduce_sum.59
  391.4 16.5 %all-reduce = (f32[1024]{0:T(1024)S(1)}, f32[1024]{0:T(1024)S(1)}) all-reduce(f32[1024]{0:T(1024)S(1)} %bitcast.60, f32[1024]{0:T(1024)S(1)} %reduce_sum.59), channel_id=1, replica_groups=mesh['cent'=8,'dp'=32] {'cent'}, use_global_device_ids=true, to_apply=%region_7.0 | all-reduce | flops 2048 | bytes 16384 | tf_op jit(solution)/shard_map/psum | solution.py:62
  407.9 4.0 multiply_convert_fusion
  412.0 0.9 divide_convert_fusion
  (13 shorter events, 0.1 us)
Async XLA Ops:
  13.5 8.3 %copy-start.1 = (bf16[1024,1024]{1,0:T(8,128)(2,1)S(1)}, bf16[1024,1024]{1,0:T(8,128)(2,1)}, u32[]{:S(2)}) copy-start(bf16[1024,1024]{1,0:T(8,128)(2,1)} %param.4) | copy-start | bytes 6291460
  13.5 183.0 %all-to-all-start = ((bf16[32,128,1024]{2,1,0:T(8,128)(2,1)}), bf16[32,128,1024]{2,1,0:T(8,128)(2,1)}, u32[]{:S(2)}, u32[]{:S(2)}) async-start(bf16[32,128,1024]{2,1,0:T(8,128)(2,1)} %bitcast.51), calls=%async_computation | async-start | bytes 16777216 | tf_op jit(solution)/shard_map/all_to_all | solution.py:52
  19.6 2.7 copy-start.2
  24.9 1.9 copy-start
  26.9 169.4 %copy-start.3 = (bf16[2,128,1024]{2,1,0:T(8,128)(2,1)S(1)}, bf16[2,128,1024]{2,1,0:T(8,128)(2,1)}, u32[]{:S(2)}) copy-start(bf16[2,128,1024]{2,1,0:T(8,128)(2,1)} %param.7) | copy-start | bytes 1572868
  208.0 180.4 %all-to-all-start.1 = ((f32[32,128,128]{2,1,0:T(8,128)}), f32[32,128,128]{2,1,0:T(8,128)S(1)}, u32[]{:S(2)}, u32[]{:S(2)}) async-start(f32[32,128,128]{2,1,0:T(8,128)} %bitcast.53), calls=%async_computation.1 | async-start | bytes 4194304 | tf_op jit(solution)/shard_map/all_to_all | solution.py:58
where the time goes:
time: 414 us; the launch traced here: 413 us
  blocking collectives  333 us (80%)
  matrix products  36.6 us (9%)
  local copies, waits for them, and re-layouts  17.1 us (4%)
  other arithmetic  13.9 us (3%)
  starting transfers between devices  11.5 us (3%)
    psum x3, blocking collectives, shards(): col_scale = 1.0 / lax.psum(col_part, 'dp')  282 us
    psum x2, blocking collectives, shards(): row_scale = 1.0 / lax.psum(row_part, 'cent')  34.2 us
    dot_general x3, matrix products, shards(): row_part = jnp.dot(expo, col_scale, precision=lax.Precision.HIGHEST)  17.3 us
    psum x1, blocking collectives, shards(): row_total = lax.psum(row_part, 'cent')  16.5 us
    scatter x1, local copies, waits for them, and re-layouts, shards(): jnp.zeros((clusters * CAP, width), jnp.bfloat16).at[slot].set(points)  10.8 us
    dot_general x3, matrix products, shards(): col_part = jnp.dot(row_scale, expo, precision=lax.Precision.HIGHEST)  10.6 us
  transfers between devices with their start and end apart: 2, of which 0 were waited for; matrix products, arithmetic and copies ran while one was open for 8% of the time, Pallas kernels for 0%

commit v1 on v0

--- a/solution.py
+++ b/solution.py
@@ -1,3 +1,4 @@
+import functools
 import jax
 import jax.numpy as jnp
 from jax import lax
@@ -7,6 +8,14 @@
 ITERS = 3
 EPS = 1e-06
 TAU = 0.05
+
+
+def proceed_run_up(xx, link_axis):
+    opened = jnp.sum(lax.all_gather(xx, link_axis), axis=0)
+    return opened
+
+
+derive_space_up = functools.partial(proceed_run_up, link_axis="cent")
 
 
 def inverse_norm(rows):
@@ -37,7 +46,7 @@
         col_scale = 1.0 / lax.psum(col_part, "dp")
         row_part = jnp.dot(expo, col_scale, precision=lax.Precision.HIGHEST)
         if step + 1 < ITERS:
-            row_scale = 1.0 / lax.psum(row_part, "cent")
+            row_scale = 1.0 / derive_space_up(row_part)
     ids = cluster_ids[:, 0]
     labels = lax.broadcasted_iota(jnp.int32, (pts_count, clusters), 1)
     onehot = ids[:, None] == labels

time: 414 us -> 433 us (1.046)
  blocking collectives: 333 us -> 352 us
    all_gather x0 -> x2, blocking collectives: none -> 53 us  [proceed_run_up(): opened = jnp.sum(lax.all_gather(xx, link_axis), axis=0)]
    psum x2 -> x0, blocking collectives: 34.2 us -> none  [shards(): row_scale = 1.0 / lax.psum(row_part, 'cent')]
where the time goes in v1:
time: 433 us; the launch traced here: 432 us
  blocking collectives  352 us (81%)
  matrix products  36.6 us (8%)
  local copies, waits for them, and re-layouts  17.1 us (4%)
  other arithmetic  13.9 us (3%)
  starting transfers between devices  11.2 us (3%)
    psum x3, blocking collectives, shards(): col_scale = 1.0 / lax.psum(col_part, 'dp')  283 us
    all_gather x2, blocking collectives, proceed_run_up(): opened = jnp.sum(lax.all_gather(xx, link_axis), axis=0)  53 us
    dot_general x3, matrix products, shards(): row_part = jnp.dot(expo, col_scale, precision=lax.Precision.HIGHEST)  17.3 us
    psum x1, blocking collectives, shards(): row_total = lax.psum(row_part, 'cent')  16.6 us
    scatter x1, local copies, waits for them, and re-layouts, shards(): jnp.zeros((clusters * CAP, width), jnp.bfloat16).at[slot].set(points)  10.8 us
    dot_general x3, matrix products, shards(): col_part = jnp.dot(row_scale, expo, precision=lax.Precision.HIGHEST)  10.6 us
  transfers between devices with their start and end apart: 2, of which 0 were waited for; matrix products, arithmetic and copies ran while one was open for 8% of the time, Pallas kernels for 0%

profile of v1, /device:TPU:0, one launch (start us, length us, event | category | flops | bytes accessed | tf_op | source)
XLA Modules:
  0.0 431.9 jit_solution(11032764606834018619)
XLA Ops:
  0.6 1.4 fusion.11
  2.0 0.7 compare_select_fusion
  2.7 10.8 %scatter_custom_fusion = bf16[4096,1024]{1,0:T(8,128)(2,1)} fusion(s32[1024]{0:T(1024)S(1)} %bitcast.56, bf16[1024,1024]{1,0:T(8,128)(2,1)} %param.4, bf16[]{:T(256)} %constant.6.clone.1), kind=kCustom, calls=%fused_computation.6 | custom fusion | bytes 8389120 | tf_op jit(solution)/shard_map/scatter | solution.py:58
  13.5 0.0 copy-start.1
  13.5 6.1 %all-to-all-start = ((bf16[32,128,1024]{2,1,0:T(8,128)(2,1)}), bf16[32,128,1024]{2,1,0:T(8,128)(2,1)}, u32[]{:S(2)}, u32[]{:S(2)}) async-start(bf16[32,128,1024]{2,1,0:T(8,128)(2,1)} %bitcast.51), calls=%async_computation | async-start | bytes 16777216 | tf_op jit(solution)/shard_map/all_to_all | solution.py:61
  19.6 0.0 copy-start.2
  19.6 2.2 multiply_reduce_fusion.1
  21.8 0.0 copy-done.1
  21.8 0.5 multiply_reduce_fusion.2
  22.3 0.0 copy-done.2
  22.3 2.6 multiply_exponential_fusion
  24.9 0.0 copy-start
  24.9 1.9 copy-done
  26.9 0.0 copy-start.3
  26.9 2.1 fusion.14
  28.9 141.6 %psum.35 = f32[1024]{0:T(1024)S(1)} all-reduce(f32[1024]{0:T(1024)S(1)} %bitcast.55), channel_id=1, replica_groups=mesh['cent'=8,'dp'=32] {'dp'}, use_global_device_ids=true, to_apply=%region_2.0 | all-reduce | flops 1024 | bytes 8192 | tf_op jit(solution)/shard_map/psum | solution.py:46
  170.5 5.8 %fusion.17 = f32[1,1024]{1,0:T(1,128)S(1)} fusion(f32[1024,1024]{1,0:T(8,128)} %copy-done, f32[1024,1]{0,1:T(1,128)S(1)} %bitcast.63), kind=kOutput, calls=%fused_computation.39 | convolution fusion | flops 12582912 | bytes 4202496 | tf_op jit(solution)/shard_map/dot_general | solution.py:47
  176.3 28.3 %all-gather = f32[8192]{0:T(1024)S(1)} all-gather(f32[1024]{0:T(1024)S(1)} %bitcast.59), channel_id=2, replica_groups=mesh['cent'=8,'dp'=32] {'cent'}, dimensions={0}, use_global_device_ids=true | all-gather | bytes 36864 | tf_op jit(solution)/shard_map/all_gather | solution.py:14
  204.6 0.0 copy-done.3
  204.6 0.2 multiply_reduce_fusion.3
  204.8 0.0 all-to-all-done
  204.9 5.1 %multiply_reduce_fusion = f32[32,128]{1,0:T(8,128)S(1)} fusion(bf16[32,128,1024]{2,1,0:T(8,128)(2,1)} %all-to-all-done), kind=kLoop, calls=%fused_computation.2 | loop fusion | flops 12578816 | bytes 8404992 | tf_op jit(solution)/shard_map/reduce_sum | solution.py:23
  210.0 0.1 rsqrt.34
  210.1 4.8 %fusion.7 = f32[32,2,64,128]{3,2,0,1:T(8,128)S(1)} fusion(bf16[32,2,64,1024]{3,2,1,0:T(8,128)(2,1)} %bitcast.16, f32[2,128]{1,0:T(2,128)S(1)} %add_rsqrt_fusion.3, f32[32,2,64]{2,0,1:T(8,128)S(1)} %copy.13, bf16[2,128,1024]{2,1,0:T(8,128)(2,1)S(1)} %copy-done.3), kind=kOutput, calls=%fused_computation.16 | convolution fusion | flops 1075314688 | bytes 11027456 | tf_op jit(solution)/shard_map/sgcd,gkd->sgck/dot_general | solution.py:64
  214.8 1.5 copy.14
  216.3 5.2 %all-to-all-start.1 = ((f32[32,128,128]{2,1,0:T(8,128)}), f32[32,128,128]{2,1,0:T(8,128)S(1)}, u32[]{:S(2)}, u32[]{:S(2)}) async-start(f32[32,128,128]{2,1,0:T(8,128)} %bitcast.53), calls=%async_computation.1 | async-start | bytes 4194304 | tf_op jit(solution)/shard_map/all_to_all | solution.py:67
  221.5 4.3 fusion.18
  225.8 78.3 %psum.36 = f32[1024]{0:T(1024)S(1)} all-reduce(f32[1024]{0:T(1024)S(1)} %bitcast.64), channel_id=1, replica_groups=mesh['cent'=8,'dp'=32] {'dp'}, use_global_device_ids=true, to_apply=%region_4.0 | all-reduce | flops 1024 | bytes 8192 | tf_op jit(solution)/shard_map/psum | solution.py:46
  304.1 5.8 %fusion.19 = f32[1,1024]{1,0:T(1,128)S(1)} fusion(f32[1024,1024]{1,0:T(8,128)} %copy-done, f32[1024,1]{0,1:T(1,128)S(1)} %bitcast.65), kind=kOutput, calls=%fused_computation.41 | convolution fusion | flops 12582912 | bytes 4202496 | tf_op jit(solution)/shard_map/dot_general | solution.py:47
  309.8 24.7 %all-gather.1 = f32[8192]{0:T(1024)S(1)} all-gather(f32[1024]{0:T(1024)S(1)} %bitcast.60), channel_id=3, replica_groups=mesh['cent'=8,'dp'=32] {'cent'}, dimensions={0}, use_global_device_ids=true | all-gather | bytes 36864 | tf_op jit(solution)/shard_map/all_gather | solution.py:14
  334.5 4.3 fusion.20
  338.8 62.7 %psum.37 = f32[1024]{0:T(1024)S(1)} all-reduce(f32[1024]{0:T(1024)S(1)} %bitcast.67), channel_id=1, replica_groups=mesh['cent'=8,'dp'=32] {'dp'}, use_global_device_ids=true, to_apply=%region_6.0 | all-reduce | flops 1024 | bytes 8192 | tf_op jit(solution)/shard_map/psum | solution.py:46
  401.5 5.8 %fusion.21 = f32[1,1024]{1,0:T(1,128)S(1)} fusion(f32[1024,1024]{1,0:T(8,128)} %copy-done, f32[1024,1]{0,1:T(1,128)S(1)} %bitcast.54), kind=kOutput, calls=%fused_computation.43 | convolution fusion | flops 12582912 | bytes 4202496 | tf_op jit(solution)/shard_map/dot_general | solution.py:47
  407.2 0.0 all-to-all-done.1
  407.2 2.8 gather_fusion
  410.1 0.2 reduce_sum.79
  410.3 16.6 %all-reduce = (f32[1024]{0:T(1024)S(1)}, f32[1024]{0:T(1024)S(1)}) all-reduce(f32[1024]{0:T(1024)S(1)} %bitcast.62, f32[1024]{0:T(1024)S(1)} %reduce_sum.79), channel_id=1, replica_groups=mesh['cent'=8,'dp'=32] {'cent'}, use_global_device_ids=true, to_apply=%region_7.0 | all-reduce | flops 2048 | bytes 16384 | tf_op jit(solution)/shard_map/psum | solution.py:71
  426.9 4.0 multiply_convert_fusion
  431.0 0.9 divide_convert_fusion
  (17 shorter events, 0.1 us)
Async XLA Ops:
  13.5 8.3 %copy-start.1 = (bf16[1024,1024]{1,0:T(8,128)(2,1)S(1)}, bf16[1024,1024]{1,0:T(8,128)(2,1)}, u32[]{:S(2)}) copy-start(bf16[1024,1024]{1,0:T(8,128)(2,1)} %param.4) | copy-start | bytes 6291460
  13.5 191.4 %all-to-all-start = ((bf16[32,128,1024]{2,1,0:T(8,128)(2,1)}), bf16[32,128,1024]{2,1,0:T(8,128)(2,1)}, u32[]{:S(2)}, u32[]{:S(2)}) async-start(bf16[32,128,1024]{2,1,0:T(8,128)(2,1)} %bitcast.51), calls=%async_computation | async-start | bytes 16777216 | tf_op jit(solution)/shard_map/all_to_all | solution.py:61
  19.6 2.7 copy-start.2
  24.9 1.9 copy-start
  26.9 177.8 %copy-start.3 = (bf16[2,128,1024]{2,1,0:T(8,128)(2,1)S(1)}, bf16[2,128,1024]{2,1,0:T(8,128)(2,1)}, u32[]{:S(2)}) copy-start(bf16[2,128,1024]{2,1,0:T(8,128)(2,1)} %param.7) | copy-start | bytes 1572868
  216.3 190.9 %all-to-all-start.1 = ((f32[32,128,128]{2,1,0:T(8,128)}), f32[32,128,128]{2,1,0:T(8,128)S(1)}, u32[]{:S(2)}, u32[]{:S(2)}) async-start(f32[32,128,128]{2,1,0:T(8,128)} %bitcast.53), calls=%async_computation.1 | async-start | bytes 4194304 | tf_op jit(solution)/shard_map/all_to_all | solution.py:67
